TPU v7x, 128 devices: a whole 4x4x4 slice. The times are simulated.
128 devices in a mesh: dp: 8 (over x, core), fsdp: 16 (over y, z).
Axes of the slice: x: 4, y: 4, z: 4, core: 2. Of those that a mesh axis runs over, the one named last changes fastest.
Arguments:
- tokens: bfloat16 [65536, 8192], P(('dp', 'fsdp')), may hold values from -6 to 6
- frozen_value_matrix: bfloat16 [8192, 1024], P('fsdp'), may hold values from -0.0625 to 0.0625
- adapter_down_maps: bfloat16 [512, 64, 8192], P('dp', None, 'fsdp'), may hold values from -0.0625 to 0.0625
- adapter_up_maps: bfloat16 [512, 64, 1024], P('dp', None, 'fsdp'), may hold values from -0.375 to 0.375
- value_output_gradient: bfloat16 [65536, 1024], P(('dp', 'fsdp')), may hold values from -0.125 to 0.125
- window_composer_position: int32 [8, 64], P('dp'), may hold values from 0 to 3
- needed_composers: int32 [8, 4], replicated, may hold values from 0 to 511, as said below
- composer_storage_index: int32 [512], replicated, may hold values from 0 to 511, as said below
Outputs:
- value: bfloat16 [65536, 1024], P(('dp', 'fsdp'))
- grad_down: float32 [512, 64, 8192], P('dp', None, 'fsdp')
- grad_up: float32 [512, 64, 1024], P('dp', None, 'fsdp')
Inputs may be any that keep to these rules, and one draw needn't show every extreme that they name: Every storage index appears once: the adapters and gradients of composer c lie at index composer_storage_index[c]; composer c is owned by index composer_storage_index[c] // 64 of dp. `needed_composers`: the 4 composers of one row have 4 different owners along dp.
All inputs are finite; a program needn't handle non-finite values.
Results may differ from a plain program's by a relative error of at most 0.004.
Values may be sent and summed in bfloat16 or wider, within the bound.
No kernel may reach another device: no remote copies, remote signals or barrier semaphores. Data moves between devices by JAX's collectives and lax.ppermute only.
A program may use at most 128 MiB of HBM per device.

v0:
```python
import jax
import jax.numpy as jnp
from jax import lax
from jax.sharding import PartitionSpec as P

WIN = 128
ADAPTER_SCALE = 2.0


def body(
    tokens,
    frozen_value_matrix,
    adapter_down_maps,
    adapter_up_maps,
    value_output_gradient,
    window_composer_position,
    needed_composers,
    composer_storage_index,
):
    f32, bf16 = (jnp.float32, jnp.bfloat16)
    dp_count = lax.axis_size("dp")
    fsdp_count = lax.axis_size("fsdp")
    group_index = lax.axis_index("dp")
    member_index = lax.axis_index("fsdp")
    tok_rows, width = tokens.shape
    value_cols = frozen_value_matrix.shape[1]
    rank = adapter_down_maps.shape[1]
    each_owner_rows = adapter_down_maps.shape[0]
    down_cols = adapter_down_maps.shape[2]
    up_cols = adapter_up_maps.shape[2]
    list_len = needed_composers.shape[1]
    windows = tok_rows // WIN
    part_cols = value_cols // dp_count
    w_part = lax.dynamic_slice_in_dim(
        frozen_value_matrix, group_index * part_cols, part_cols, axis=1
    )
    w_part_full = lax.all_gather(w_part, "fsdp", axis=0, tiled=True)
    up_x = [(i, (i + 2) % dp_count) for i in range(dp_count)]
    down_x = [(i, (i - 2) % dp_count) for i in range(dp_count)]
    from_left = lax.ppermute(w_part_full, "dp", up_x)
    from_right = lax.ppermute(w_part_full, "dp", down_x)
    half_part = part_cols // 2
    far_a = lax.ppermute(from_left[:, :half_part], "dp", up_x)
    far_b = lax.ppermute(from_right[:, half_part:], "dp", down_x)
    far = jnp.concatenate([far_a, far_b], axis=1)
    same_parity = [w_part_full, from_left, far, from_right]
    w_own = jnp.concatenate(same_parity, axis=1)
    w_partner = lax.ppermute(w_own, "dp", [(i, i ^ 1) for i in range(dp_count)])
    out_own = jnp.dot(tokens, w_own, preferred_element_type=f32)
    out_partner = jnp.dot(tokens, w_partner, preferred_element_type=f32)
    held = jnp.concatenate([out_own, out_partner], axis=1).reshape(tok_rows, dp_count, part_cols)
    part_ids = jnp.arange(dp_count, dtype=jnp.int32)
    partner_index = group_index ^ 1
    same = part_ids % 2 == group_index % 2
    where_held = jnp.where(
        same,
        (group_index - part_ids) % dp_count // 2,
        dp_count // 2 + (partner_index - part_ids) % dp_count // 2,
    )
    frozen_rows = jnp.take(held, where_held, axis=1).reshape(tok_rows, value_cols)
    list_slot = jnp.take(composer_storage_index, needed_composers, axis=0)
    list_owner = list_slot // each_owner_rows
    list_local = list_slot % each_owner_rows
    owned_here = list_owner == group_index
    locally_owned_slots = jnp.sum(jnp.where(owned_here, list_local, 0), axis=1)
    owned_any = jnp.any(owned_here, axis=1)
    send = jnp.concatenate(
        [
            jnp.take(adapter_down_maps, locally_owned_slots, axis=0),
            jnp.take(adapter_up_maps, locally_owned_slots, axis=0),
        ],
        axis=2,
    )
    send = jnp.where(owned_any[:, None, None], send, jnp.zeros((), send.dtype))
    got = lax.all_to_all(send, "dp", split_axis=0, concat_axis=0, tiled=True)
    my_owner = lax.dynamic_index_in_dim(list_owner, group_index, 0, keepdims=False)
    slab = jnp.take(got, my_owner, axis=0)
    shares = lax.all_gather(slab, "fsdp", axis=0, tiled=False)
    full_down = shares[..., :down_cols].transpose(1, 2, 0, 3).reshape(list_len, rank, width)
    full_up = shares[..., down_cols:].transpose(1, 2, 0, 3).reshape(list_len, rank, value_cols)
    group_picks = window_composer_position[0]
    my_picks = lax.dynamic_slice_in_dim(group_picks, member_index * windows, windows, 0)
    slot_range = jnp.arange(list_len, dtype=jnp.int32)
    token_hot = jnp.broadcast_to(
        my_picks[:, None, None] == slot_range[None, None, :], (windows, WIN, list_len)
    ).reshape(tok_rows, list_len)
    hot_f = token_hot.astype(f32)
    down_flat = full_down.reshape(list_len * rank, width)
    up_flat = full_up.reshape(list_len * rank, value_cols)
    low_all = lax.dot_general(
        tokens, down_flat, (((1,), (1,)), ((), ())), preferred_element_type=f32
    ).reshape(tok_rows, list_len, rank)
    low = jnp.sum(low_all * hot_f[:, :, None], axis=1).astype(bf16)
    hot_h = token_hot.astype(bf16)
    masked_low = (hot_h[:, :, None] * low[:, None, :]).reshape(tok_rows, list_len * rank)
    adapter_change = jnp.dot(masked_low, up_flat, preferred_element_type=f32)
    value = (frozen_rows + ADAPTER_SCALE * adapter_change).astype(bf16)
    back_all = lax.dot_general(
        value_output_gradient, up_flat, (((1,), (1,)), ((), ())), preferred_element_type=f32
    ).reshape(tok_rows, list_len, rank)
    back = (ADAPTER_SCALE * jnp.sum(back_all * hot_f[:, :, None], axis=1)).astype(bf16)
    masked_back = (hot_h[:, :, None] * back[:, None, :]).reshape(tok_rows, list_len * rank)
    scaled_masked_low = masked_low * jnp.asarray(ADAPTER_SCALE, bf16)
    contract = (((0,), (0,)), ((), ()))
    part_down = lax.dot_general(masked_back, tokens, contract, preferred_element_type=f32)
    part_up = lax.dot_general(
        scaled_masked_low, value_output_gradient, contract, preferred_element_type=f32
    )
    rows = list_len * rank
    up_rows = rows * up_cols // down_cols
    up_as_rows = (
        part_up.reshape(rows, fsdp_count, up_cols)
        .transpose(1, 0, 2)
        .reshape(fsdp_count, up_rows, down_cols)
        .transpose(1, 0, 2)
        .reshape(up_rows, fsdp_count * down_cols)
    )
    both = jnp.concatenate([part_down, up_as_rows], axis=0)
    summed = lax.psum_scatter(both, "fsdp", scatter_dimension=1, tiled=True)
    per_slot = jnp.concatenate(
        [
            summed[:rows].reshape(list_len, rank, down_cols),
            summed[rows:].reshape(list_len, up_rows // list_len, down_cols),
        ],
        axis=1,
    )
    owner_range = jnp.arange(dp_count, dtype=jnp.int32)
    to_owner = my_owner[None, :] == owner_range[:, None]
    pick_index = jnp.sum(jnp.where(to_owner, slot_range[None, :], 0), axis=1)
    owner_has = jnp.any(to_owner, axis=1)
    send_grad = jnp.take(per_slot, pick_index, axis=0)
    send_grad = jnp.where(owner_has[:, None, None], send_grad, 0.0)
    back_grad = lax.all_to_all(send_grad, "dp", split_axis=0, concat_axis=0, tiled=True)
    land = jnp.where(owned_any, locally_owned_slots, 0)
    arrived = jnp.where(owned_any[:, None, None], back_grad, 0.0)
    grad_down = jnp.zeros((each_owner_rows, rank, down_cols), f32).at[land].add(arrived[:, :rank])
    grad_up = (
        jnp.zeros((each_owner_rows, rank, up_cols), f32)
        .at[land]
        .add(arrived[:, rank:].reshape(dp_count, rank, up_cols))
    )
    return (value, grad_down, grad_up)


def solution(mesh):
    return jax.shard_map(
        body,
        mesh=mesh,
        in_specs=(
            P(("dp", "fsdp"), None),
            P("fsdp", None),
            P("dp", None, "fsdp"),
            P("dp", None, "fsdp"),
            P(("dp", "fsdp"), None),
            P("dp", None),
            P(),
            P(),
        ),
        out_specs=(P(("dp", "fsdp"), None), P("dp", None, "fsdp"), P("dp", None, "fsdp")),
        check_vma=False,
    )
```

profile of v0, /device:TPU:1, one launch (start us, length us, event | category | flops | bytes accessed | tf_op | source)
XLA Modules:
  0.0 275.7 jit_solution(16079173203989045500)
XLA Ops:
  10.0 1.8 gather_fusion.3
  11.8 2.8 %gather_fusion.2 = bf16[8,64,512]{2,1,0:T(8,128)(2,1)S(1)} fusion(bf16[64,64,512]{2,1,0:T(8,128)(2,1)} %param.10, s32[1024]{0:T(1024)S(1)} %pad_clamp_fusion.2), kind=kCustom, calls=%fused_computation.2 | custom fusion | bytes 1048608 | tf_op jit(solution)/shard_map/jit(_take)/gather | solution.py:69
  15.9 5.8 %all-to-all-start = ((bf16[8,64,576]{2,1,0:T(8,128)(2,1)}), bf16[8,64,576]{2,1,0:T(8,128)(2,1)S(1)}, u32[]{:S(2)}, u32[]{:S(2)}) async-start(bf16[8,64,576]{2,1,0:T(8,128)(2,1)} %maximum_select_fusion), calls=%async_computation | async-start | bytes 1310720 | tf_op jit(solution)/shard_map/all_to_all | solution.py:75
  21.7 10.9 %all-to-all-done = bf16[8,64,576]{2,1,0:T(8,128)(2,1)S(1)} async-done(((bf16[8,64,576]{2,1,0:T(8,128)(2,1)}), bf16[8,64,576]{2,1,0:T(8,128)(2,1)S(1)}, u32[]{:S(2)}, u32[]{:S(2)}) %all-to-all-start) | async-done | bytes 589856 | tf_op jit(solution)/shard_map/all_to_all | solution.py:75
  35.8 55.6 %all-gather.5.cloned.1.call-done = bf16[16,4,64,576]{3,2,1,0:T(8,128)(2,1)} async-done(((bf16[1,4,64,576]{3,2,1,0:T(8,128)(2,1)}), bf16[16,4,64,576]{3,2,1,0:T(8,128)(2,1)}) %all-gather.5.cloned.1.call-update) | async-done | bytes 4718608 | tf_op jit(solution)/shard_map/all_gather | solution.py:78
  92.7 1.7 copy.33
  94.4 2.1 reshape_reshape.7
  96.5 2.9 %slice_bitcast_fusion = bf16[4,64,16,512]{3,1,0,2:T(8,128)(2,1)S(1)} fusion(bf16[16,4,64,576]{3,2,1,0:T(8,128)(2,1)} %all-gather.5.cloned.1.call-done), kind=kLoop, calls=%fused_computation.9 | loop fusion | bytes 8388608 | tf_op jit(solution)/shard_map/transpose | solution.py:79
  99.9 2.4 copy.32
  102.3 4.4 %copy.44 = bf16[32,8,16,512]{3,1,2,0:T(8,128)(2,1)S(1)} copy(bf16[32,8,16,512]{3,2,1,0:T(8,128)(2,1)S(1)} %bitcast.101) | data formatting | bytes 8388608
  106.7 2.4 fusion.20
  111.1 1.5 reshape.428
  113.9 9.4 %fusion.22 = f32[256,8192]{1,0:T(8,128)} fusion(bf16[512,256]{0,1:T(8,128)(2,1)S(1)} %bitcast.112, bf16[512,8192]{1,0:T(8,128)(2,1)} %param.8), kind=kOutput, calls=%fused_computation.127 | convolution fusion | flops 2147483648 | bytes 17039360 | tf_op jit(solution)/shard_map/dot_general | solution.py:105
  123.3 8.2 %pad_maximum_fusion = f32[288,8192]{1,0:T(8,128)} fusion(f32[32,8192]{1,0:T(8,128)S(1)} %bitcast.107, f32[256,8192]{1,0:T(8,128)} %fusion.22), kind=kLoop, calls=%fused_computation.8 | loop fusion | flops 2359296 | bytes 18874368 | tf_op jit(solution)/shard_map/concatenate | solution.py:118
  131.5 9.2 %all-gather.3.cloned.1.call-done = bf16[8192,128]{0,1:T(8,128)(2,1)} async-done(((bf16[512,128]{0,1:T(8,128)(2,1)}), bf16[8192,128]{0,1:T(8,128)(2,1)}) %all-gather.3.cloned.1.call-update) | async-done | bytes 2097168 | tf_op jit(solution)/shard_map/all_gather | solution.py:37
  141.9 1.5 collective-permute-start.2
  143.4 44.4 %collective-permute-done = bf16[8192,128]{0,1:T(8,128)(2,1)S(1)} collective-permute-done((bf16[8192,128]{0,1:T(8,128)(2,1)}, bf16[8192,128]{0,1:T(8,128)(2,1)S(1)}, u32[]{:S(2)}, u32[]{:S(2)}) %collective-permute-start) | collective-permute-done | bytes 2097184 | tf_op jit(solution)/shard_map/ppermute | solution.py:40
  188.0 3.2 %constant_dynamic-update-slice_fusion.4 = bf16[8192,512]{0,1:T(8,128)(2,1)} fusion(bf16[8192,128]{0,1:T(8,128)(2,1)} %all-gather.3.cloned.1.call-done), kind=kLoop, calls=%fused_computation.35 | loop fusion | bytes 4194304
  191.3 2.7 collective-permute-start.3
  194.0 1.5 constant_dynamic-update-slice_fusion.3
  195.5 16.0 %collective-permute-done.1 = bf16[8192,64]{0,1:T(8,128)(2,1)S(1)} collective-permute-done((bf16[8192,64]{0,1:T(8,128)(2,1)S(1)}, bf16[8192,64]{0,1:T(8,128)(2,1)S(1)}, u32[]{:S(2)}, u32[]{:S(2)}) %collective-permute-start.1) | collective-permute-done | bytes 1048608 | tf_op jit(solution)/shard_map/ppermute | solution.py:43
  212.5 1.5 collective-permute-done.3
  215.0 1.5 constant_dynamic-update-slice_fusion
  216.5 3.4 %collective-permute-start.4 = (bf16[8192,512]{0,1:T(8,128)(2,1)}, bf16[8192,512]{0,1:T(8,128)(2,1)}, u32[]{:S(2)}, u32[]{:S(2)}) collective-permute-start(bf16[8192,512]{0,1:T(8,128)(2,1)} %constant_dynamic-update-slice_fusion), channel_id=1, source_target_pairs={{0,16},{16,0},{32,48},{48,32},{64,80},{80,64},{96,112},{112,96},{1... | collective-permute-start | bytes 25165832 | tf_op jit(solution)/shard_map/ppermute | solution.py:48
  220.2 11.5 %convolution_bitcast_fusion.2 = f32[512,512]{0,1:T(8,128)} fusion(bf16[8192,512]{0,1:T(8,128)(2,1)} %constant_dynamic-update-slice_fusion, bf16[512,8192]{1,0:T(8,128)(2,1)} %param.8), kind=kOutput, calls=%fused_computation.14 | convolution fusion | flops 4294967296 | bytes 17825792 | tf_op jit(solution)/shard_map/dot_general | solution.py:49
  235.6 5.1 %all-to-all-start.1 = ((f32[8,72,512]{2,1,0:T(8,128)}), f32[8,72,512]{2,1,0:T(8,128)}, u32[]{:S(2)}, u32[]{:S(2)}) async-start(f32[8,72,512]{2,1,0:T(8,128)} %select_select_fusion), calls=%async_computation.2 | async-start | bytes 2359296 | tf_op jit(solution)/shard_map/all_to_all | solution.py:133
  240.7 9.6 %convolution_bitcast_fusion.1 = f32[512,512]{0,1:T(8,128)S(1)} fusion(bf16[8192,512]{0,1:T(8,128)(2,1)} %collective-permute-done.4, bf16[512,8192]{1,0:T(8,128)(2,1)} %param.8), kind=kOutput, calls=%fused_computation.13 | convolution fusion | flops 4294967296 | bytes 17825792 | tf_op jit(solution)/shard_map/dot_general | solution.py:50
  250.5 2.0 gather_fusion
  252.5 1.9 copy.39
  257.3 1.5 broadcast_select_fusion
  259.0 4.5 %broadcast_in_dim.151 = f32[64,64,512]{2,1,0:T(8,128)} broadcast(f32[]{:T(128)} %constant.200.clone.1), dimensions={} | broadcast | bytes 8388612 | tf_op jit(solution)/shard_map/broadcast_in_dim | solution.py:136
  263.5 3.2 %scatter_fusion = f32[64,64,512]{2,1,0:T(8,128)} fusion(f32[64,64,512]{2,1,0:T(8,128)} %broadcast_in_dim.151, s32[8]{0:T(128)S(1)} %get-tuple-element.13, f32[8,64,512]{2,1,0:T(8,128)S(1)} %slice.50), kind=kCustom, calls=%fused_computation.6 | custom fusion | flops 262144 | bytes 3145760 | tf_op jit(solution)/shard_map/scatter-add | solution.py:136
  (95 shorter events, 25.6 us)
Async XLA Ops:
  7.2 26.9 %copy-start = (bf16[512,1024]{1,0:T(8,128)(2,1)S(1)}, bf16[512,1024]{1,0:T(8,128)(2,1)}, u32[]{:S(2)}) copy-start(bf16[512,1024]{1,0:T(8,128)(2,1)} %param.9) | copy-start | bytes 3145732
  9.5 25.5 %copy-start.8 = (s32[1,64]{1,0:T(1,128)S(1)}, s32[1,64]{1,0:T(1,128)}, u32[]{:S(2)}) copy-start(s32[1,64]{1,0:T(1,128)} %param.13) | copy-start | bytes 772
  9.5 25.7 %copy-start.4 = (bf16[512,1024]{1,0:T(8,128)(2,1)S(1)}, bf16[512,1024]{1,0:T(8,128)(2,1)}, u32[]{:S(2)}) copy-start(bf16[512,1024]{1,0:T(8,128)(2,1)} %param.12) | copy-start | bytes 3145732
  15.9 16.7 %all-to-all-start = ((bf16[8,64,576]{2,1,0:T(8,128)(2,1)}), bf16[8,64,576]{2,1,0:T(8,128)(2,1)S(1)}, u32[]{:S(2)}, u32[]{:S(2)}) async-start(bf16[8,64,576]{2,1,0:T(8,128)(2,1)} %maximum_select_fusion), calls=%async_computation | async-start | bytes 1310720 | tf_op jit(solution)/shard_map/all_to_all | solution.py:75
  21.7 69.7 %all-gather.5.cloned.1.call-start = ((), (), s32[]{:S(2)}) async-start(), calls=%async_computation.4 | async-start | bytes 5570560 | tf_op jit(solution)/shard_map/all_gather | solution.py:78
  34.0 106.7 %all-gather.3.cloned.1.call-start = ((), (), s32[]{:S(2)}) async-start(), calls=%async_computation.3 | async-start | bytes 2228224 | tf_op jit(solution)/shard_map/all_gather | solution.py:37
  35.0 196.7 %reduce-scatter.2.cloned.1.call-start = ((), (), s32[]{:S(2)}) async-start(), calls=%async_computation.5 | async-start | bytes 10027008 | tf_op jit(solution)/shard_map/reduce_scatter | solution.py:119
  96.5 3.4 %copy-start.2 = (bf16[256,1024]{1,0:T(8,128)(2,1)}, bf16[256,1024]{1,0:T(8,128)(2,1)S(1)}, u32[]{:S(2)}) copy-start(bf16[256,1024]{1,0:T(8,128)(2,1)S(1)} %reshape_reshape.7) | copy-start | bytes 1572868
  99.9 6.8 %slice-start = ((s8[8388608]{0:T(1024)(128)(4,1)}), s8[4194304]{0:T(1024)(128)(4,1)S(1)}, s32[]{:S(2)}) async-start(s8[8388608]{0:T(1024)(128)(4,1)} %bitcast.103), calls=%async_computation.6 | async-start | bytes 8388608
  102.3 4.4 %slice-start.1 = ((s8[8388608]{0:T(1024)(128)(4,1)}), s8[4194304]{0:T(1024)(128)(4,1)S(1)}, s32[]{:S(2)}) async-start(s8[8388608]{0:T(1024)(128)(4,1)} %bitcast.103), calls=%async_computation.7 | async-start | bytes 8388608
  140.7 47.1 %collective-permute-start = (bf16[8192,128]{0,1:T(8,128)(2,1)}, bf16[8192,128]{0,1:T(8,128)(2,1)S(1)}, u32[]{:S(2)}, u32[]{:S(2)}) collective-permute-start(bf16[8192,128]{0,1:T(8,128)(2,1)} %all-gather.3.cloned.1.call-done), channel_id=1, source_target_pairs={{0,32},{16,48},{32,64},{48,80},{64,96},{80,112},{96,0},{112,16},{1... | collective-permute-start | bytes 6291464 | tf_op jit(solution)/shard_map/ppermute | solution.py:40
  141.9 49.3 %collective-permute-start.2 = (bf16[8192,128]{0,1:T(8,128)(2,1)}, bf16[8192,128]{0,1:T(8,128)(2,1)S(1)}, u32[]{:S(2)}, u32[]{:S(2)}) collective-permute-start(bf16[8192,128]{0,1:T(8,128)(2,1)} %all-gather.3.cloned.1.call-done), channel_id=1, source_target_pairs={{0,96},{16,112},{32,0},{48,16},{64,32},{80,48},{96,64},{112,80},{1... | collective-permute-start | bytes 6291464 | tf_op jit(solution)/shard_map/ppermute | solution.py:41
  187.9 23.6 %collective-permute-start.1 = (bf16[8192,64]{0,1:T(8,128)(2,1)S(1)}, bf16[8192,64]{0,1:T(8,128)(2,1)S(1)}, u32[]{:S(2)}, u32[]{:S(2)}) collective-permute-start(bf16[8192,64]{0,1:T(8,128)(2,1)S(1)} %slice.44), channel_id=1, source_target_pairs={{0,32},{16,48},{32,64},{48,80},{64,96},{80,112},{96,0},{112,16},{1... | collective-permute-start | bytes 3145736 | tf_op jit(solution)/shard_map/ppermute | solution.py:43
  191.3 22.7 %collective-permute-start.3 = (bf16[8192,64]{0,1:T(8,128)(2,1)S(1)}, bf16[8192,64]{0,1:T(8,128)(2,1)S(1)}, u32[]{:S(2)}, u32[]{:S(2)}) collective-permute-start(bf16[8192,64]{0,1:T(8,128)(2,1)S(1)} %slice.45), channel_id=1, source_target_pairs={{0,96},{16,112},{32,0},{48,16},{64,32},{80,48},{96,64},{112,80},{1... | collective-permute-start | bytes 3145736 | tf_op jit(solution)/shard_map/ppermute | solution.py:44
  216.5 24.3 %collective-permute-start.4 = (bf16[8192,512]{0,1:T(8,128)(2,1)}, bf16[8192,512]{0,1:T(8,128)(2,1)}, u32[]{:S(2)}, u32[]{:S(2)}) collective-permute-start(bf16[8192,512]{0,1:T(8,128)(2,1)} %constant_dynamic-update-slice_fusion), channel_id=1, source_target_pairs={{0,16},{16,0},{32,48},{48,32},{64,80},{80,64},{96,112},{112,96},{1... | collective-permute-start | bytes 25165832 | tf_op jit(solution)/shard_map/ppermute | solution.py:48
  235.6 21.8 %all-to-all-start.1 = ((f32[8,72,512]{2,1,0:T(8,128)}), f32[8,72,512]{2,1,0:T(8,128)}, u32[]{:S(2)}, u32[]{:S(2)}) async-start(f32[8,72,512]{2,1,0:T(8,128)} %select_select_fusion), calls=%async_computation.2 | async-start | bytes 2359296 | tf_op jit(solution)/shard_map/all_to_all | solution.py:133
  240.7 9.6 %copy-start.7 = (f32[512,512]{0,1:T(8,128)S(1)}, f32[512,512]{0,1:T(8,128)}, u32[]{:S(2)}) copy-start(f32[512,512]{0,1:T(8,128)} %convolution_bitcast_fusion.2) | copy-start | bytes 3145732
  250.5 4.0 %copy-start.3 = (bf16[256,1024]{1,0:T(8,128)(2,1)S(1)}, bf16[256,1024]{1,0:T(8,128)(2,1)}, u32[]{:S(2)}) copy-start(bf16[256,1024]{1,0:T(8,128)(2,1)} %copy-done.2) | copy-start | bytes 1572868
  250.5 4.0 %copy-start.6 = (bf16[512,4,64]{0,2,1:T(8,128)(2,1)S(1)}, bf16[512,4,64]{0,2,1:T(8,128)(2,1)}, u32[]{:S(2)}) copy-start(bf16[512,4,64]{0,2,1:T(8,128)(2,1)} %get-tuple-element.11) | copy-start | bytes 786436
  259.0 10.2 %copy-start.1 = (bf16[512,1024]{1,0:T(8,128)(2,1)S(1)}, bf16[512,1024]{1,0:T(8,128)(2,1)}, u32[]{:S(2)}) copy-start(bf16[512,1024]{1,0:T(8,128)(2,1)} %param.9) | copy-start | bytes 3145732
  267.9 1.3 copy-start.5
Sparse Core Ops, SparseCore 0:
  34.2 57.1 all-gather.4
  94.1 46.5 all-gather.2
  144.2 86.6 reduce-scatter.1
where the time goes:
time: 276 us
  waiting for transfers between devices  139 us (50%)
  local copies, waits for them, and re-layouts  48.5 us (18%)
  matrix products  35.2 us (13%)
  starting transfers between devices  20 us (7%)
  other arithmetic  18.9 us (7%)
  between operations  14.2 us (5%)
    all_gather x1, waiting for transfers between devices, body(): shares = lax.all_gather(slab, 'fsdp', axis=0, tiled=False)  55.6 us
    ppermute x1, waiting for transfers between devices, body(): from_left = lax.ppermute(w_part_full, 'dp', up_x)  44.4 us
    ppermute x1, waiting for transfers between devices, body(): far_a = lax.ppermute(from_left[:, :half_part], 'dp', up_x)  16 us
    unnamed x34, local copies, waits for them, and re-layouts  14.8 us
    dot_general x1, matrix products, body(): out_own = jnp.dot(tokens, w_own, preferred_element_type=f32)  11.5 us
    all_to_all x1, waiting for transfers between devices, body(): got = lax.all_to_all(send, 'dp', split_axis=0, concat_axis=0, tiled=True)  10.9 us
    dot_general x1, matrix products, body(): out_partner = jnp.dot(tokens, w_partner, preferred_element_type=f32)  9.59 us
    dot_general x1, matrix products, body(): lax.dot_general(masked_back, tokens, contract, preferred_element_type=f32)  9.36 us
  transfers between devices with their start and end apart: 10, of which 7 were waited for; matrix products, arithmetic and copies ran while one was open for 29% of the time, Pallas kernels for 0%

commit v1 on v0

--- a/solution.py
+++ b/solution.py
@@ -34,7 +34,9 @@
     w_part = lax.dynamic_slice_in_dim(
         frozen_value_matrix, group_index * part_cols, part_cols, axis=1
     )
-    w_part_full = lax.all_gather(w_part, "fsdp", axis=0, tiled=True)
+    w_part_full = jnp.concatenate(
+        lax.all_to_all(jnp.stack([w_part] * lax.axis_size("fsdp")), "fsdp", 0, 0), axis=0
+    )
     up_x = [(i, (i + 2) % dp_count) for i in range(dp_count)]
     down_x = [(i, (i - 2) % dp_count) for i in range(dp_count)]
     from_left = lax.ppermute(w_part_full, "dp", up_x)

time: 276 us -> 331 us (1.20)
  blocking collectives: 0 us -> 41.2 us
  local copies, waits for them, and re-layouts: 48.5 us -> 71.9 us
  waiting for transfers between devices: 139 us -> 124 us
  starting transfers between devices: 20 us -> 23.7 us
    all_to_all x0 -> x1, blocking collectives: none -> 41.2 us  [body(): lax.all_to_all(jnp.stack([w_part] * lax.axis_size('fsdp')), 'fsdp', 0, 0)]
    concatenate x1, local copies, waits for them, and re-layouts: 1.46 us -> 14.4 us  [body(): w_own = jnp.concatenate(same_parity, axis=1)]
    all_gather x1 -> x0, waiting for transfers between devices: 9.21 us -> none  [body(): w_part_full = lax.all_gather(w_part, 'fsdp', axis=0, tiled=True)]
    unnamed x34 -> x33, local copies, waits for them, and re-layouts: 14.8 us -> 8.6 us
    slice x1 -> x2, local copies, waits for them, and re-layouts: 0.07 us -> 6.29 us  [body(): far_b = lax.ppermute(from_right[:, half_part:], 'dp', down_x)]
    ppermute x1, waiting for transfers between devices: 16 us -> 11 us  [body(): far_a = lax.ppermute(from_left[:, :half_part], 'dp', up_x)]
    ppermute x0 -> x2, local copies, waits for them, and re-layouts: none -> 4.59 us  [the longest x1 2.72 us: body(): far_b = lax.ppermute(from_right[:, half_part:], 'dp', down_x)]
    ppermute x1, waiting for transfers between devices: 44.4 us -> 40.5 us  [body(): from_left = lax.ppermute(w_part_full, 'dp', up_x)]
  transfers between devices with their start and end apart: 10 -> 9, of which waited for: 7 -> 6; matrix products, arithmetic and copies ran while one was open for 29% -> 19% of each run, Pallas kernels for 0% -> 0%
where the time goes in v1:
time: 331 us; the launch traced here: 330 us
  waiting for transfers between devices  124 us (37%)
  local copies, waits for them, and re-layouts  71.9 us (22%)
  blocking collectives  41.2 us (12%)
  matrix products  36.2 us (11%)
  starting transfers between devices  23.7 us (7%)
  other arithmetic  18.7 us (6%)
  between operations  14.5 us (4%)
    all_gather x1, waiting for transfers between devices, body(): shares = lax.all_gather(slab, 'fsdp', axis=0, tiled=False)  56.5 us
    all_to_all x1, blocking collectives, body(): lax.all_to_all(jnp.stack([w_part] * lax.axis_size('fsdp')), 'fsdp', 0, 0)  41.2 us
    ppermute x1, waiting for transfers between devices, body(): from_left = lax.ppermute(w_part_full, 'dp', up_x)  40.5 us
    concatenate x1, local copies, waits for them, and re-layouts, body(): w_own = jnp.concatenate(same_parity, axis=1)  14.4 us
    dot_general x1, matrix products, body(): out_own = jnp.dot(tokens, w_own, preferred_element_type=f32)  11.3 us
    ppermute x1, waiting for transfers between devices, body(): far_a = lax.ppermute(from_left[:, :half_part], 'dp', up_x)  11 us
    all_to_all x1, waiting for transfers between devices, body(): got = lax.all_to_all(send, 'dp', split_axis=0, concat_axis=0, tiled=True)  10.9 us
    dot_general x1, matrix products, body(): out_partner = jnp.dot(tokens, w_partner, preferred_element_type=f32)  9.61 us
  transfers between devices with their start and end apart: 9, of which 6 were waited for; matrix products, arithmetic and copies ran while one was open for 19% of the time, Pallas kernels for 0%

profile of v1, /device:TPU:1, one launch (start us, length us, event | category | flops | bytes accessed | tf_op | source)
XLA Modules:
  0.0 329.8 jit_solution(3641484779301759075)
XLA Ops:
  11.2 2.8 gather_fusion.2
  15.2 5.8 %all-to-all-start.1 = ((bf16[8,64,576]{2,1,0:T(8,128)(2,1)}), bf16[8,64,576]{2,1,0:T(8,128)(2,1)S(1)}, u32[]{:S(2)}, u32[]{:S(2)}) async-start(bf16[8,64,576]{2,1,0:T(8,128)(2,1)} %maximum_select_fusion), calls=%async_computation.1 | async-start | bytes 1310720 | tf_op jit(solution)/shard_map/all_to_all | solution.py:77
  21.1 10.9 %all-to-all-done.1 = bf16[8,64,576]{2,1,0:T(8,128)(2,1)S(1)} async-done(((bf16[8,64,576]{2,1,0:T(8,128)(2,1)}), bf16[8,64,576]{2,1,0:T(8,128)(2,1)S(1)}, u32[]{:S(2)}, u32[]{:S(2)}) %all-to-all-start.1) | async-done | bytes 589856 | tf_op jit(solution)/shard_map/all_to_all | solution.py:77
  34.3 56.5 %all-gather.2.cloned.1.call-done = bf16[16,4,64,576]{3,2,1,0:T(8,128)(2,1)} async-done(((bf16[1,4,64,576]{3,2,1,0:T(8,128)(2,1)}), bf16[16,4,64,576]{3,2,1,0:T(8,128)(2,1)}) %all-gather.2.cloned.1.call-update) | async-done | bytes 4718608 | tf_op jit(solution)/shard_map/all_gather | solution.py:80
  93.7 2.1 reshape_reshape.7
  97.8 2.7 slice_bitcast_fusion
  100.5 2.4 copy.59
  102.9 4.4 %copy.70 = bf16[32,8,16,512]{3,1,2,0:T(8,128)(2,1)S(1)} copy(bf16[32,8,16,512]{3,2,1,0:T(8,128)(2,1)S(1)} %bitcast.103) | data formatting | bytes 8388608
  107.3 2.4 fusion.20
  111.1 1.9 copy.63
  113.0 2.2 reshape.434
  115.2 9.1 %fusion.22 = f32[256,8192]{1,0:T(8,128)} fusion(bf16[512,256]{0,1:T(8,128)(2,1)S(1)} %bitcast.118, bf16[512,8192]{1,0:T(8,128)(2,1)} %param.8), kind=kOutput, calls=%fused_computation.122 | convolution fusion | flops 2147483648 | bytes 17039360 | tf_op jit(solution)/shard_map/dot_general | solution.py:107
  124.4 8.0 %pad_maximum_fusion = f32[288,8192]{1,0:T(8,128)} fusion(f32[32,8192]{1,0:T(8,128)S(1)} %bitcast.113, f32[256,8192]{1,0:T(8,128)} %fusion.22), kind=kLoop, calls=%fused_computation.8 | loop fusion | flops 2359296 | bytes 18874368 | tf_op jit(solution)/shard_map/concatenate | solution.py:120
  132.8 41.2 %all_to_all.15 = bf16[16,512,128]{1,2,0:T(8,128)(2,1)} all-to-all(bf16[16,512,128]{1,2,0:T(8,128)(2,1)S(1)} %stack.2), channel_id=1, replica_groups=mesh['dp'=8,'fsdp'=16] {'fsdp'}, dimensions={0} | all-to-all | bytes 4194304 | tf_op jit(solution)/shard_map/all_to_all | solution.py:38
  174.0 3.1 copy.50
  179.8 40.5 %collective-permute-done = bf16[8192,128]{1,0:T(8,128)(2,1)S(1)} collective-permute-done((bf16[8192,128]{1,0:T(8,128)(2,1)S(1)}, bf16[8192,128]{1,0:T(8,128)(2,1)S(1)}, u32[]{:S(2)}, u32[]{:S(2)}) %collective-permute-start) | collective-permute-done | bytes 2097184 | tf_op jit(solution)/shard_map/ppermute | solution.py:42
  221.6 2.7 copy.51
  224.3 3.6 %slice.45 = bf16[8192,64]{1,0:T(8,128)(2,1)} slice(bf16[8192,128]{1,0:T(8,128)(2,1)} %collective-permute-done.2), slice={[0:8192], [64:128]} | slice | bytes 2097152 | tf_op jit(solution)/shard_map/slice | solution.py:46
  227.9 2.7 copy.52
  230.6 2.7 collective-permute-start.3
  233.2 11.0 %collective-permute-done.1 = bf16[8192,64]{0,1:T(8,128)(2,1)S(1)} collective-permute-done((bf16[8192,64]{0,1:T(8,128)(2,1)}, bf16[8192,64]{0,1:T(8,128)(2,1)S(1)}, u32[]{:S(2)}, u32[]{:S(2)}) %collective-permute-start.1) | collective-permute-done | bytes 1048608 | tf_op jit(solution)/shard_map/ppermute | solution.py:45
  246.1 3.5 %collective-permute-done.3 = bf16[8192,64]{0,1:T(8,128)(2,1)} collective-permute-done((bf16[8192,64]{0,1:T(8,128)(2,1)}, bf16[8192,64]{0,1:T(8,128)(2,1)}, u32[]{:S(2)}, u32[]{:S(2)}) %collective-permute-start.3) | collective-permute-done | bytes 1048608 | tf_op jit(solution)/shard_map/ppermute | solution.py:46
  249.6 2.7 copy.54
  252.3 14.4 %concatenate.15 = bf16[8192,512]{1,0:T(8,128)(2,1)} concatenate(bf16[8192,128]{1,0:T(8,128)(2,1)S(1)} %bitcast.107, bf16[8192,128]{1,0:T(8,128)(2,1)} %copy-done.3, bf16[8192,64]{1,0:T(8,128)(2,1)} %copy.53, bf16[8192,64]{1,0:T(8,128)(2,1)} %copy.54, bf16[8192,128]{1,0:T(8,128)(2,1)} %collective-permute-done.2), dimensions={1} | concatenate | bytes 16777216 | tf_op jit(solution)/shard_map/concatenate | solution.py:49
  266.7 7.3 %collective-permute-start.4 = (bf16[8192,512]{1,0:T(8,128)(2,1)}, bf16[8192,512]{1,0:T(8,128)(2,1)}, u32[]{:S(2)}, u32[]{:S(2)}) collective-permute-start(bf16[8192,512]{1,0:T(8,128)(2,1)} %concatenate.15), channel_id=1, source_target_pairs={{0,16},{16,0},{32,48},{48,32},{64,80},{80,64},{96,112},{112,96},{1... | collective-permute-start | bytes 25165832 | tf_op jit(solution)/shard_map/ppermute | solution.py:50
  274.3 11.3 %convolution_bitcast_fusion.2 = f32[512,512]{0,1:T(8,128)} fusion(bf16[8192,512]{1,0:T(8,128)(2,1)} %concatenate.15, bf16[512,8192]{1,0:T(8,128)(2,1)} %param.8), kind=kOutput, calls=%fused_computation.14 | convolution fusion | flops 4294967296 | bytes 17825792 | tf_op jit(solution)/shard_map/dot_general | solution.py:51
  289.5 5.1 %all-to-all-start.2 = ((f32[8,72,512]{2,1,0:T(8,128)}), f32[8,72,512]{2,1,0:T(8,128)}, u32[]{:S(2)}, u32[]{:S(2)}) async-start(f32[8,72,512]{2,1,0:T(8,128)} %select_select_fusion), calls=%async_computation.3 | async-start | bytes 2359296 | tf_op jit(solution)/shard_map/all_to_all | solution.py:135
  294.5 9.6 %convolution_bitcast_fusion.1 = f32[512,512]{0,1:T(8,128)S(1)} fusion(bf16[8192,512]{1,0:T(8,128)(2,1)} %collective-permute-done.4, bf16[512,8192]{1,0:T(8,128)(2,1)} %param.8), kind=kOutput, calls=%fused_computation.13 | convolution fusion | flops 4294967296 | bytes 17825792 | tf_op jit(solution)/shard_map/dot_general | solution.py:52
  304.3 2.0 gather_fusion
  306.4 2.0 copy.66
  312.8 4.5 %broadcast_in_dim.151 = f32[64,64,512]{2,1,0:T(8,128)} broadcast(f32[]{:T(128)} %constant.200.clone.1), dimensions={} | broadcast | bytes 8388612 | tf_op jit(solution)/shard_map/broadcast_in_dim | solution.py:138
  317.3 3.2 scatter_fusion
  (98 shorter events, 31.3 us)
Async XLA Ops:
  7.2 125.2 %copy-start = (bf16[512,1024]{1,0:T(8,128)(2,1)S(1)}, bf16[512,1024]{1,0:T(8,128)(2,1)}, u32[]{:S(2)}) copy-start(bf16[512,1024]{1,0:T(8,128)(2,1)} %param.9) | copy-start | bytes 3145732
  7.2 1.0 copy-start.2
  14.2 19.3 %copy-start.10 = (s32[1,64]{1,0:T(1,128)S(1)}, s32[1,64]{1,0:T(1,128)}, u32[]{:S(2)}) copy-start(s32[1,64]{1,0:T(1,128)} %param.13) | copy-start | bytes 772
  14.2 19.5 %copy-start.6 = (bf16[512,1024]{1,0:T(8,128)(2,1)S(1)}, bf16[512,1024]{1,0:T(8,128)(2,1)}, u32[]{:S(2)}) copy-start(bf16[512,1024]{1,0:T(8,128)(2,1)} %param.12) | copy-start | bytes 3145732
  15.2 16.7 %all-to-all-start.1 = ((bf16[8,64,576]{2,1,0:T(8,128)(2,1)}), bf16[8,64,576]{2,1,0:T(8,128)(2,1)S(1)}, u32[]{:S(2)}, u32[]{:S(2)}) async-start(bf16[8,64,576]{2,1,0:T(8,128)(2,1)} %maximum_select_fusion), calls=%async_computation.1 | async-start | bytes 1310720 | tf_op jit(solution)/shard_map/all_to_all | solution.py:77
  21.0 69.7 %all-gather.2.cloned.1.call-start = ((), (), s32[]{:S(2)}) async-start(), calls=%async_computation.4 | async-start | bytes 5570560 | tf_op jit(solution)/shard_map/all_gather | solution.py:80
  33.4 252.2 %reduce-scatter.2.cloned.1.call-start = ((), (), s32[]{:S(2)}) async-start(), calls=%async_computation.5 | async-start | bytes 10027008 | tf_op jit(solution)/shard_map/reduce_scatter | solution.py:121
  95.9 4.6 %copy-start.4 = (bf16[256,1024]{1,0:T(8,128)(2,1)}, bf16[256,1024]{1,0:T(8,128)(2,1)S(1)}, u32[]{:S(2)}) copy-start(bf16[256,1024]{1,0:T(8,128)(2,1)S(1)} %reshape_reshape.7) | copy-start | bytes 1572868
  100.5 6.8 %slice-start = ((s8[8388608]{0:T(1024)(128)(4,1)}), s8[4194304]{0:T(1024)(128)(4,1)S(1)}, s32[]{:S(2)}) async-start(s8[8388608]{0:T(1024)(128)(4,1)} %bitcast.109), calls=%async_computation.6 | async-start | bytes 8388608
  102.9 4.4 %slice-start.1 = ((s8[8388608]{0:T(1024)(128)(4,1)}), s8[4194304]{0:T(1024)(128)(4,1)S(1)}, s32[]{:S(2)}) async-start(s8[8388608]{0:T(1024)(128)(4,1)} %bitcast.109), calls=%async_computation.7 | async-start | bytes 8388608
  177.0 43.2 %collective-permute-start = (bf16[8192,128]{1,0:T(8,128)(2,1)S(1)}, bf16[8192,128]{1,0:T(8,128)(2,1)S(1)}, u32[]{:S(2)}, u32[]{:S(2)}) collective-permute-start(bf16[8192,128]{1,0:T(8,128)(2,1)S(1)} %bitcast.105), channel_id=1, source_target_pairs={{0,32},{16,48},{32,64},{48,80},{64,96},{80,112},{96,0},{112,16},{1... | collective-permute-start | bytes 6291464 | tf_op jit(solution)/shard_map/ppermute | solution.py:42
  178.3 46.0 %collective-permute-start.2 = (bf16[8192,128]{1,0:T(8,128)(2,1)S(1)}, bf16[8192,128]{1,0:T(8,128)(2,1)}, u32[]{:S(2)}, u32[]{:S(2)}) collective-permute-start(bf16[8192,128]{1,0:T(8,128)(2,1)S(1)} %bitcast.106), channel_id=1, source_target_pairs={{0,96},{16,112},{32,0},{48,16},{64,32},{80,48},{96,64},{112,80},{1... | collective-permute-start | bytes 6291464 | tf_op jit(solution)/shard_map/ppermute | solution.py:43
  220.3 1.3 copy-start.3
  224.3 20.0 %collective-permute-start.1 = (bf16[8192,64]{0,1:T(8,128)(2,1)}, bf16[8192,64]{0,1:T(8,128)(2,1)S(1)}, u32[]{:S(2)}, u32[]{:S(2)}) collective-permute-start(bf16[8192,64]{0,1:T(8,128)(2,1)} %copy.51), channel_id=1, source_target_pairs={{0,32},{16,48},{32,64},{48,80},{64,96},{80,112},{96,0},{112,16},{1... | collective-permute-start | bytes 3145736 | tf_op jit(solution)/shard_map/ppermute | solution.py:45
  230.6 19.0 %collective-permute-start.3 = (bf16[8192,64]{0,1:T(8,128)(2,1)}, bf16[8192,64]{0,1:T(8,128)(2,1)}, u32[]{:S(2)}, u32[]{:S(2)}) collective-permute-start(bf16[8192,64]{0,1:T(8,128)(2,1)} %copy.52), channel_id=1, source_target_pairs={{0,96},{16,112},{32,0},{48,16},{64,32},{80,48},{96,64},{112,80},{1... | collective-permute-start | bytes 3145736 | tf_op jit(solution)/shard_map/ppermute | solution.py:46
  266.7 27.8 %collective-permute-start.4 = (bf16[8192,512]{1,0:T(8,128)(2,1)}, bf16[8192,512]{1,0:T(8,128)(2,1)}, u32[]{:S(2)}, u32[]{:S(2)}) collective-permute-start(bf16[8192,512]{1,0:T(8,128)(2,1)} %concatenate.15), channel_id=1, source_target_pairs={{0,16},{16,0},{32,48},{48,32},{64,80},{80,64},{96,112},{112,96},{1... | collective-permute-start | bytes 25165832 | tf_op jit(solution)/shard_map/ppermute | solution.py:50
  289.5 21.7 %all-to-all-start.2 = ((f32[8,72,512]{2,1,0:T(8,128)}), f32[8,72,512]{2,1,0:T(8,128)}, u32[]{:S(2)}, u32[]{:S(2)}) async-start(f32[8,72,512]{2,1,0:T(8,128)} %select_select_fusion), calls=%async_computation.3 | async-start | bytes 2359296 | tf_op jit(solution)/shard_map/all_to_all | solution.py:135
  294.5 9.6 %copy-start.9 = (f32[512,512]{0,1:T(8,128)S(1)}, f32[512,512]{0,1:T(8,128)}, u32[]{:S(2)}) copy-start(f32[512,512]{0,1:T(8,128)} %convolution_bitcast_fusion.2) | copy-start | bytes 3145732
  306.3 2.0 copy-start.5
  306.4 2.0 copy-start.8
  317.3 5.7 %copy-start.1 = (bf16[512,1024]{1,0:T(8,128)(2,1)S(1)}, bf16[512,1024]{1,0:T(8,128)(2,1)}, u32[]{:S(2)}) copy-start(bf16[512,1024]{1,0:T(8,128)(2,1)} %param.9) | copy-start | bytes 3145732
  321.7 1.3 copy-start.7
Sparse Core Ops, SparseCore 0:
  33.5 57.1 all-gather.1
  132.5 101.0 reduce-scatter.1
